TPU v7x, 128 devices: a whole 4x4x4 slice. The times are simulated.
128 devices in a mesh: grp: 8 (over y, core), shard: 16 (over z, x).
Axes of the slice: x: 4, y: 4, z: 4, core: 2. Of those that a mesh axis runs over, the one named last changes fastest.
Arguments:
- tokens: bfloat16 [65536, 2560], P(('grp', 'shard')), may hold values from -6 to 6
- gain: float32 [2560], replicated, may hold values from 0.25 to 1.75
- w_qkv: bfloat16 [2560, 3072], P(None, 'shard'), may hold values from -1 to 1
- prefix_kv: bfloat16 [8, 2048, 512], P('grp', 'shard'), may hold values from -6 to 6
- prefix_owner: int32 [8], P('grp'), may hold values from 0 to 7, as said below
- suffix_len: int32 [8, 16], P('grp', 'shard'), may hold values from 1 to 512, 5120 in all within a row
- slots: int32 [8, 8192], P('grp', 'shard'), may hold values from 0 to 8191, as said below
Outputs:
- attended: bfloat16 [65536, 2560], P(('grp', 'shard'))
Inputs may be any that keep to these rules, and one draw needn't show every extreme that they name: In each group the slots are a permutation of 0 to 8191; in each aligned run of 512 entries the k-th block of 32 entries holds slots k * 512 to (k + 1) * 512 - 1. `suffix_len`: each group's lengths sum to 5120 and one of them equals 512. `prefix_owner`: each entry names one of the 8 caches; several groups may name the same one.
All inputs are finite; a program needn't handle non-finite values.
Results may differ from a plain program's by a relative error of at most 0.0069.
Values may be sent and summed in bfloat16 or wider, within the bound.
No kernel may reach another device: no remote copies, remote signals or barrier semaphores. Data moves between devices by JAX's collectives and lax.ppermute only.
A program may use at most 128 MiB of HBM per device.

v0:
```python
import jax
import jax.numpy as jnp
from jax import lax
from jax.experimental import pallas as pl
from jax.experimental.pallas import tpu as pltpu
from jax.sharding import PartitionSpec as P


H = 10
HD = 256
WINDOW = 2048
TQ = 256


def normalize(rows, gain):
    rows32 = rows.astype(jnp.float32)
    factor = lax.rsqrt(jnp.mean(rows32 * rows32, axis=-1, keepdims=True) + 1e-06)
    return (rows32 * factor * gain).astype(jnp.bfloat16)


def _attn_kernel(len_ref, q_ref, pk_ref, pv_ref, sk_ref, sv_ref, o_ref, s_ref, p_ref):
    n = len_ref[0]
    pre = pk_ref.shape[0]
    count = q_ref.shape[0]
    nt = (((1,), (1,)), ((), ()))
    for i in range(count // TQ):
        r0 = i * TQ
        lp = pre - r0
        ns = r0 + TQ
        q = q_ref[r0:r0 + TQ, :] * jnp.asarray(HD ** (-0.5), q_ref.dtype)
        qpos = r0 + lax.broadcasted_iota(jnp.int32, (TQ, 1), 0)
        s_ref[:, :lp] = lax.dot_general(q, pk_ref[r0:, :], nt, preferred_element_type=jnp.float32)
        s_ref[:, lp:lp + ns] = lax.dot_general(q, sk_ref[:ns, :], nt, preferred_element_type=jnp.float32)
        ppos = r0 + lax.broadcasted_iota(jnp.int32, (1, TQ), 1)
        vis_p = (ppos > pre + qpos - WINDOW) & (ppos <= pre + qpos) & (ppos < pre + n)
        s_ref[:, :TQ] = jnp.where(vis_p, s_ref[:, :TQ], -1e30)
        spos = pre + lax.broadcasted_iota(jnp.int32, (1, ns), 1)
        vis_s = (spos > pre + qpos - WINDOW) & (spos <= pre + qpos) & (spos < pre + n)
        s_ref[:, lp:lp + ns] = jnp.where(vis_s, s_ref[:, lp:lp + ns], -1e30)
        s = s_ref[:, :lp + ns]
        top = jnp.max(s, axis=-1, keepdims=True)
        e = jnp.exp(s - top)
        s_ref[...] = e
        inv = 1.0 / jnp.sum(e, axis=-1, keepdims=True)
        p_ref[...] = (s_ref[...] * inv).astype(p_ref.dtype)
        acc = jnp.dot(p_ref[:, :lp], pv_ref[r0:, :], preferred_element_type=jnp.float32)
        out = acc + jnp.dot(p_ref[:, lp:lp + ns], sv_ref[:ns, :], preferred_element_type=jnp.float32)
        o_ref[r0:r0 + TQ, :] = jnp.where(qpos < n, out, 0.0).astype(o_ref.dtype)


def attend(qkv, prefix, length):
    count = qkv.shape[0]
    pre = prefix.shape[0]
    width = pre + TQ
    grid_spec = pltpu.PrefetchScalarGridSpec(
        num_scalar_prefetch=1,
        grid=(H,),
        in_specs=[
            pl.BlockSpec((count, HD), lambda h, n: (0, h)),
            pl.BlockSpec((pre, HD), lambda h, n: (0, 0)),
            pl.BlockSpec((pre, HD), lambda h, n: (0, 1)),
            pl.BlockSpec((count, HD), lambda h, n: (0, H)),
            pl.BlockSpec((count, HD), lambda h, n: (0, H + 1)),
        ],
        out_specs=pl.BlockSpec((count, HD), lambda h, n: (0, h)),
        scratch_shapes=[
            pltpu.VMEM((TQ, width), jnp.float32),
            pltpu.VMEM((TQ, width), jnp.bfloat16),
        ],
    )
    flops = 4 * H * count * width * HD
    return pl.pallas_call(
        _attn_kernel,
        out_shape=jax.ShapeDtypeStruct((count, H * HD), jnp.bfloat16),
        grid_spec=grid_spec,
        compiler_params=pltpu.CompilerParams(vmem_limit_bytes=48 * 1024 * 1024),
        cost_estimate=pl.CostEstimate(
            flops=flops,
            transcendentals=H * count * width,
            bytes_accessed=2 * (count * qkv.shape[1] + pre * prefix.shape[1] + count * H * HD),
        ),
    )(length.reshape(1).astype(jnp.int32), qkv, prefix, prefix, qkv, qkv)


def gather_by_a2a(piece, axis_name, count):
    spread = jnp.broadcast_to(piece[None], (count,) + piece.shape)
    return lax.all_to_all(spread, axis_name, 0, 0, tiled=True)


def shards(tokens, gain, w_qkv, prefix_kv, prefix_owner, suffix_len, slots):
    tok_dev = tokens.shape[0]
    n_grp = lax.axis_size("grp")
    n_shard = lax.axis_size("shard")
    core = lax.axis_index("grp") % 2
    pairs = [(g, g ^ 1) for g in range(n_grp)]

    here = slots.reshape(tok_dev, 1) % tok_dev
    code = jnp.concatenate([here // 32, here % 32], axis=1).astype(tokens.dtype)
    code = jnp.pad(code, ((0, 0), (0, 126)))
    arrived = lax.all_to_all(jnp.concatenate([tokens, code], axis=1), "shard", 0, 0, tiled=True)
    local_prefix, arrived = lax.optimization_barrier((prefix_kv[0], arrived))
    owner = prefix_owner[0]
    sliced = gather_by_a2a(local_prefix, "grp", n_grp)
    chosen = lax.dynamic_index_in_dim(sliced, owner, 0, keepdims=False)
    prefix = gather_by_a2a(chosen, "shard", n_shard).reshape(-1, chosen.shape[-1])
    d = tokens.shape[1]
    pos = arrived[:, d].astype(jnp.int32) * 32 + arrived[:, d + 1].astype(jnp.int32)
    onehot = (jnp.arange(tok_dev, dtype=jnp.int32)[:, None] == pos[None, :]).astype(jnp.bfloat16)
    placed = jnp.dot(onehot, arrived, preferred_element_type=jnp.float32).astype(jnp.bfloat16)[:, :d]
    normed = normalize(placed, gain)

    d = w_qkv.shape[0]
    kh = d // 2
    kc = kh // 2
    acc = None
    for part in range(2):
        w_part = lax.dynamic_slice_in_dim(w_qkv, core * kh + part * kc, kc, axis=0)
        w_rows = lax.all_gather(w_part, "shard", axis=1, tiled=True)
        w_other = lax.ppermute(w_rows, "grp", pairs)
        n_mine = lax.dynamic_slice_in_dim(normed, core * kh + part * kc, kc, axis=1)
        n_other = lax.dynamic_slice_in_dim(normed, (1 - core) * kh + part * kc, kc, axis=1)
        term = jnp.dot(n_mine, w_rows, preferred_element_type=jnp.float32)
        term = term + jnp.dot(n_other, w_other, preferred_element_type=jnp.float32)
        acc = term if acc is None else acc + term
    qkv = acc.astype(jnp.bfloat16)

    lengths = suffix_len.reshape(-1)
    return attend(qkv, prefix, lengths[0])


def solution(mesh):
    return jax.shard_map(
        shards,
        mesh=mesh,
        in_specs=(
            P(("grp", "shard"), None),
            P(),
            P(None, "shard"),
            P("grp", "shard", None),
            P("grp"),
            P("grp", "shard"),
            P("grp", "shard"),
        ),
        out_specs=P(("grp", "shard"), None),
        check_vma=False,
    )
```

profile of v0, /device:TPU:0, one launch (start us, length us, event | category | flops | bytes accessed | tf_op | source)
XLA Modules:
  0.0 242.5 jit_solution(11426198075070635853)
XLA Ops:
  6.5 0.0 all-gather.3.cloned.1.call-start
  6.5 1.9 constant_dynamic-slice_fusion.1
  8.4 0.0 all-gather.3.cloned.1.call-update
  8.5 0.0 all-gather.5.cloned.1.call-start
  8.5 0.7 all-gather.5.cloned.1.call-update
  9.2 0.7 fusion.18
  10.0 0.2 copy.13
  10.2 3.5 %fusion.4 = bf16[512,2688]{1,0:T(8,128)(2,1)} fusion(bf16[512,2]{1,0:T(8,128)(2,1)S(1)} %copy.13, bf16[512,2560]{1,0:T(8,128)(2,1)} %param.7), kind=kLoop, calls=%fused_computation.9 | loop fusion | flops 8257536 | bytes 5376000 | tf_op jit(solution)/shard_map/concatenate | solution.py:100
  13.6 8.0 %all-to-all-start = ((bf16[16,32,2688]{2,1,0:T(8,128)(2,1)}), bf16[16,32,2688]{2,1,0:T(8,128)(2,1)S(1)}, u32[]{:S(2)}, u32[]{:S(2)}) async-start(bf16[16,32,2688]{2,1,0:T(8,128)(2,1)} %bitcast.22), calls=%async_computation | async-start | bytes 5505024 | tf_op jit(solution)/shard_map/all_to_all | solution.py:100
  21.6 0.0 copy-start.1
  21.6 67.6 %all-gather.3.cloned.1.call-done = bf16[640,3072]{0,1:T(8,128)(2,1)} async-done(((bf16[640,192]{0,1:T(8,128)(2,1)}), bf16[640,3072]{0,1:T(8,128)(2,1)}) %all-gather.3.cloned.1.call-update) | async-done | bytes 3932176 | tf_op jit(solution)/shard_map/all_gather | solution.py:118
  89.3 0.0 collective-permute-start
  89.3 52.0 %all-gather.5.cloned.1.call-done = bf16[640,3072]{0,1:T(8,128)(2,1)} async-done(((bf16[640,192]{0,1:T(8,128)(2,1)}), bf16[640,3072]{0,1:T(8,128)(2,1)}) %all-gather.5.cloned.1.call-update) | async-done | bytes 3932176 | tf_op jit(solution)/shard_map/all_gather | solution.py:118
  141.3 0.0 collective-permute-start.1
  142.6 0.0 all-to-all-done
  142.6 2.8 %copy.11 = bf16[512,2688]{0,1:T(8,128)(2,1)} copy(bf16[512,2688]{1,0:T(8,128)(2,1)S(1)} %bitcast.20) | data formatting | bytes 5505024 | tf_op jit(solution)/shard_map/optimization_barrier | solution.py:101
  145.4 0.0 copy-done.1
  145.4 1.1 broadcast_in_dim.6
  146.5 4.4 %all-to-all-start.1 = ((bf16[8,128,512]{2,1,0:T(8,128)(2,1)}), bf16[8,128,512]{2,1,0:T(8,128)(2,1)}, u32[]{:S(2)}, u32[]{:S(2)}) async-start(bf16[8,128,512]{2,1,0:T(8,128)(2,1)} %broadcast_in_dim.6), calls=%async_computation.1 | async-start | bytes 2097152 | tf_op jit(solution)/shard_map/all_to_all | solution.py:87
  150.9 0.8 fusion.16
  151.6 0.0 copy-start.2
  151.6 1.7 fusion.5
  153.3 0.6 fusion.1
  153.9 0.0 copy-done.2
  153.9 0.7 fusion.3
  154.6 0.0 copy-start
  154.6 12.3 %all-to-all-done.1 = bf16[8,128,512]{2,1,0:T(8,128)(2,1)} async-done(((bf16[8,128,512]{2,1,0:T(8,128)(2,1)}), bf16[8,128,512]{2,1,0:T(8,128)(2,1)}, u32[]{:S(2)}, u32[]{:S(2)}) %all-to-all-start.1) | async-done | bytes 1048608 | tf_op jit(solution)/shard_map/all_to_all | solution.py:87
  166.9 0.9 dynamic-slice_bitcast_fusion
  167.8 1.5 broadcast_in_dim.8
  169.3 5.1 %all-to-all-start.2 = ((bf16[16,128,512]{2,1,0:T(8,128)(2,1)}), bf16[16,128,512]{2,1,0:T(8,128)(2,1)}, u32[]{:S(2)}, u32[]{:S(2)}) async-start(bf16[16,128,512]{2,1,0:T(8,128)(2,1)} %broadcast_in_dim.8), calls=%async_computation.2 | async-start | bytes 4194304 | tf_op jit(solution)/shard_map/all_to_all | solution.py:87
  174.4 0.0 copy-start.3
  174.4 4.9 %fusion.11 = f32[512,3072]{1,0:T(8,128)S(1)} fusion(bf16[640,3072]{0,1:T(8,128)(2,1)} %all-gather.3.cloned.1.call-done, bf16[512,2560]{1,0:T(8,128)(2,1)S(1)} %fusion.3, s32[]{:T(128)S(6)} %select_n.72), kind=kOutput, calls=%fused_computation.17 | convolution fusion | flops 2013265920 | bytes 10878980 | tf_op jit(solution)/shard_map/dot_general | solution.py:122
  179.3 0.0 copy-done.3
  179.3 4.6 %fusion.7 = f32[512,3072]{1,0:T(8,128)} fusion(bf16[640,3072]{0,1:T(8,128)(2,1)S(1)} %copy-done.3, bf16[512,2560]{1,0:T(8,128)(2,1)S(1)} %fusion.3, s32[]{:T(128)S(6)} %select_n.74), kind=kOutput, calls=%fused_computation.13 | convolution fusion | flops 2013265920 | bytes 10878980 | tf_op jit(solution)/shard_map/dot_general | solution.py:122
  183.9 0.0 collective-permute-done
  183.9 0.0 copy-done
  183.9 6.7 %fusion.9 = f32[512,3072]{1,0:T(8,128)} fusion(bf16[640,3072]{0,1:T(8,128)(2,1)} %collective-permute-done, bf16[512,2560]{1,0:T(8,128)(2,1)S(1)} %fusion.3, s32[]{:T(128)S(6)} %select_n.73), kind=kOutput, calls=%fused_computation.15 | convolution fusion | flops 2013265920 | bytes 10878980 | tf_op jit(solution)/shard_map/dot_general | solution.py:123
  190.6 0.0 collective-permute-done.1
  190.6 8.7 %add_convert_fusion.q_ref.sk_ref.sv_ref = bf16[512,3072]{1,0:T(8,128)(2,1)S(1)} fusion(f32[512,3072]{1,0:T(8,128)} %fusion.7, f32[512,3072]{1,0:T(8,128)S(1)} %fusion.11, f32[512,3072]{1,0:T(8,128)} %fusion.9, bf16[640,3072]{0,1:T(8,128)(2,1)} %collective-permute-done.1, bf16[512,2560]{1,0:T(8,128)(2,1)} %copy-done, s32[]{:T(128)S(6)} %select_n.75), kind=kOutput, calls=%fused_computation.2 | convolution fusion | flops 2019557376 | bytes 26607620 | tf_op jit(solution)/shard_map/dot_general | solution.py:123
  199.3 6.1 %all-to-all-done.2 = bf16[16,128,512]{2,1,0:T(8,128)(2,1)} async-done(((bf16[16,128,512]{2,1,0:T(8,128)(2,1)}), bf16[16,128,512]{2,1,0:T(8,128)(2,1)}, u32[]{:S(2)}, u32[]{:S(2)}) %all-to-all-start.2) | async-done | bytes 2097184 | tf_op jit(solution)/shard_map/all_to_all | solution.py:87
  205.4 30.2 %shard_map.73 = bf16[512,2560]{1,0:T(8,128)(2,1)} custom-call(s32[1]{0:T(128)} %bitcast.19.len_ref, bf16[512,3072]{1,0:T(8,128)(2,1)S(1)} %add_convert_fusion.q_ref.sk_ref.sv_ref, bf16[2048,512]{1,0:T(8,128)(2,1)} %bitcast.8.pk_ref.pv_ref, bf16[2048,512]{1,0:T(8,128)(2,1)} %bitcast.8.pk_ref.pv_ref, ...), custom_call_target="tpu_custom_call" | custom-call | flops 12079595520 | bytes 7864320 | tf_op jit(solution)/shard_map/pallas_call | solution.py:72
  (3 shorter events, 0.0 us)
Async XLA Ops:
  6.5 82.7 %all-gather.3.cloned.1.call-start = ((), (), s32[]{:S(2)}) async-start(), calls=%async_computation.3 | async-start | bytes 4177920 | tf_op jit(solution)/shard_map/all_gather | solution.py:118
  8.5 132.8 %all-gather.5.cloned.1.call-start = ((), (), s32[]{:S(2)}) async-start(), calls=%async_computation.4 | async-start | bytes 4177920 | tf_op jit(solution)/shard_map/all_gather | solution.py:118
  13.6 129.0 %all-to-all-start = ((bf16[16,32,2688]{2,1,0:T(8,128)(2,1)}), bf16[16,32,2688]{2,1,0:T(8,128)(2,1)S(1)}, u32[]{:S(2)}, u32[]{:S(2)}) async-start(bf16[16,32,2688]{2,1,0:T(8,128)(2,1)} %bitcast.22), calls=%async_computation | async-start | bytes 5505024 | tf_op jit(solution)/shard_map/all_to_all | solution.py:100
  21.6 123.8 %copy-start.1 = (bf16[1,128,512]{2,1,0:T(8,128)(2,1)S(1)}, bf16[1,128,512]{2,1,0:T(8,128)(2,1)}, u32[]{:S(2)}) copy-start(bf16[1,128,512]{2,1,0:T(8,128)(2,1)} %param.10) | copy-start | bytes 393220
  89.3 94.7 %collective-permute-start = (bf16[640,3072]{0,1:T(8,128)(2,1)}, bf16[640,3072]{0,1:T(8,128)(2,1)}, u32[]{:S(2)}, u32[]{:S(2)}) collective-permute-start(bf16[640,3072]{0,1:T(8,128)(2,1)} %all-gather.3.cloned.1.call-done), channel_id=1, source_target_pairs={{0,16},{16,0},{32,48},{48,32},{64,80},{80,64},{96,112},{112,96},{1... | collective-permute-start | bytes 11796488 | tf_op jit(solution)/shard_map/ppermute | solution.py:119
  141.3 49.3 %collective-permute-start.1 = (bf16[640,3072]{0,1:T(8,128)(2,1)}, bf16[640,3072]{0,1:T(8,128)(2,1)}, u32[]{:S(2)}, u32[]{:S(2)}) collective-permute-start(bf16[640,3072]{0,1:T(8,128)(2,1)} %all-gather.5.cloned.1.call-done), channel_id=1, source_target_pairs={{0,16},{16,0},{32,48},{48,32},{64,80},{80,64},{96,112},{112,96},{1... | collective-permute-start | bytes 11796488 | tf_op jit(solution)/shard_map/ppermute | solution.py:119
  146.5 20.4 %all-to-all-start.1 = ((bf16[8,128,512]{2,1,0:T(8,128)(2,1)}), bf16[8,128,512]{2,1,0:T(8,128)(2,1)}, u32[]{:S(2)}, u32[]{:S(2)}) async-start(bf16[8,128,512]{2,1,0:T(8,128)(2,1)} %broadcast_in_dim.6), calls=%async_computation.1 | async-start | bytes 2097152 | tf_op jit(solution)/shard_map/all_to_all | solution.py:87
  151.6 2.3 copy-start.2
  154.6 29.4 %copy-start = (bf16[512,2560]{1,0:T(8,128)(2,1)}, bf16[512,2560]{1,0:T(8,128)(2,1)S(1)}, u32[]{:S(2)}) copy-start(bf16[512,2560]{1,0:T(8,128)(2,1)S(1)} %fusion.3) | copy-start | bytes 7864324
  169.3 36.1 %all-to-all-start.2 = ((bf16[16,128,512]{2,1,0:T(8,128)(2,1)}), bf16[16,128,512]{2,1,0:T(8,128)(2,1)}, u32[]{:S(2)}, u32[]{:S(2)}) async-start(bf16[16,128,512]{2,1,0:T(8,128)(2,1)} %broadcast_in_dim.8), calls=%async_computation.2 | async-start | bytes 4194304 | tf_op jit(solution)/shard_map/all_to_all | solution.py:87
  174.4 4.9 %copy-start.3 = (bf16[640,3072]{0,1:T(8,128)(2,1)S(1)}, bf16[640,3072]{0,1:T(8,128)(2,1)}, u32[]{:S(2)}) copy-start(bf16[640,3072]{0,1:T(8,128)(2,1)} %all-gather.5.cloned.1.call-done) | copy-start | bytes 11796484
Sparse Core Ops, SparseCore 0:
  9.5 79.7 all-gather.2
  91.4 49.8 all-gather.4
where the time goes:
time: 243 us
  waiting for transfers between devices  139 us (57%)
  Pallas kernels  30.2 us (12%)
  matrix products  26.6 us (11%)
  starting transfers between devices  17.5 us (7%)
  between operations  14.8 us (6%)
  local copies, waits for them, and re-layouts  8.37 us (3%)
  other arithmetic  6.24 us (3%)
    all_gather x2, waiting for transfers between devices, shards(): w_rows = lax.all_gather(w_part, 'shard', axis=1, tiled=True)  120 us
    pallas_call x1, Pallas kernels, attend(): pl.pallas_call(_attn_kernel, out_shape=jax.ShapeDtypeStruct((count, H * H...  30.2 us
    all_to_all x2, waiting for transfers between devices, gather_by_a2a(): return lax.all_to_all(spread, axis_name, 0, 0, tiled=True)  18.4 us
    dot_general x2, matrix products, shards(): term = term + jnp.dot(n_other, w_other, preferred_element_type=jnp.float32)  15.4 us
    dot_general x2, matrix products, shards(): term = jnp.dot(n_mine, w_rows, preferred_element_type=jnp.float32)  9.51 us
    all_to_all x2, starting transfers between devices, gather_by_a2a(): return lax.all_to_all(spread, axis_name, 0, 0, tiled=True)  9.46 us
    all_to_all x1, starting transfers between devices, shards(): lax.all_to_all(jnp.concatenate([tokens, code], axis=1), 'shard', 0, 0, ti...  7.99 us
  transfers between devices with their start and end apart: 7, of which 4 were waited for; matrix products, arithmetic and copies ran while one was open for 16% of the time, Pallas kernels for 0%

commit v1 on v0

--- a/solution.py
+++ b/solution.py
@@ -9,7 +9,7 @@
 H = 10
 HD = 256
 WINDOW = 2048
-TQ = 256
+TQ = 128
 
 
 def normalize(rows, gain):
@@ -20,17 +20,16 @@
 
 def _attn_kernel(len_ref, q_ref, pk_ref, pv_ref, sk_ref, sv_ref, o_ref, s_ref, p_ref):
     n = len_ref[0]
-    pre = pk_ref.shape[0]
+    pre = pk_ref.shape[1]
     count = q_ref.shape[0]
-    nt = (((1,), (1,)), ((), ()))
     for i in range(count // TQ):
         r0 = i * TQ
         lp = pre - r0
         ns = r0 + TQ
         q = q_ref[r0:r0 + TQ, :] * jnp.asarray(HD ** (-0.5), q_ref.dtype)
         qpos = r0 + lax.broadcasted_iota(jnp.int32, (TQ, 1), 0)
-        s_ref[:, :lp] = lax.dot_general(q, pk_ref[r0:, :], nt, preferred_element_type=jnp.float32)
-        s_ref[:, lp:lp + ns] = lax.dot_general(q, sk_ref[:ns, :], nt, preferred_element_type=jnp.float32)
+        s_ref[:, :lp] = jnp.dot(q, pk_ref[:, r0:], preferred_element_type=jnp.float32)
+        s_ref[:, lp:lp + ns] = jnp.dot(q, sk_ref[:, :ns], preferred_element_type=jnp.float32)
         ppos = r0 + lax.broadcasted_iota(jnp.int32, (1, TQ), 1)
         vis_p = (ppos > pre + qpos - WINDOW) & (ppos <= pre + qpos) & (ppos < pre + n)
         s_ref[:, :TQ] = jnp.where(vis_p, s_ref[:, :TQ], -1e30)
@@ -52,14 +51,16 @@
     count = qkv.shape[0]
     pre = prefix.shape[0]
     width = pre + TQ
+    keys_pre = prefix[:, :HD].T
+    keys_suf = qkv[:, H * HD:(H + 1) * HD].T
     grid_spec = pltpu.PrefetchScalarGridSpec(
         num_scalar_prefetch=1,
         grid=(H,),
         in_specs=[
             pl.BlockSpec((count, HD), lambda h, n: (0, h)),
-            pl.BlockSpec((pre, HD), lambda h, n: (0, 0)),
+            pl.BlockSpec((HD, pre), lambda h, n: (0, 0)),
             pl.BlockSpec((pre, HD), lambda h, n: (0, 1)),
-            pl.BlockSpec((count, HD), lambda h, n: (0, H)),
+            pl.BlockSpec((HD, count), lambda h, n: (0, 0)),
             pl.BlockSpec((count, HD), lambda h, n: (0, H + 1)),
         ],
         out_specs=pl.BlockSpec((count, HD), lambda h, n: (0, h)),
@@ -79,7 +80,7 @@
             transcendentals=H * count * width,
             bytes_accessed=2 * (count * qkv.shape[1] + pre * prefix.shape[1] + count * H * HD),
         ),
-    )(length.reshape(1).astype(jnp.int32), qkv, prefix, prefix, qkv, qkv)
+    )(length.reshape(1).astype(jnp.int32), qkv, keys_pre, prefix, keys_suf, qkv)
 
 
 def gather_by_a2a(piece, axis_name, count):
@@ -94,15 +95,15 @@
     core = lax.axis_index("grp") % 2
     pairs = [(g, g ^ 1) for g in range(n_grp)]
 
+    owner = prefix_owner[0]
+    sliced = gather_by_a2a(prefix_kv[0], "grp", n_grp)
+    chosen = lax.dynamic_index_in_dim(sliced, owner, 0, keepdims=False)
+    prefix = gather_by_a2a(chosen, "shard", n_shard).reshape(-1, chosen.shape[-1])
+
     here = slots.reshape(tok_dev, 1) % tok_dev
     code = jnp.concatenate([here // 32, here % 32], axis=1).astype(tokens.dtype)
     code = jnp.pad(code, ((0, 0), (0, 126)))
     arrived = lax.all_to_all(jnp.concatenate([tokens, code], axis=1), "shard", 0, 0, tiled=True)
-    local_prefix, arrived = lax.optimization_barrier((prefix_kv[0], arrived))
-    owner = prefix_owner[0]
-    sliced = gather_by_a2a(local_prefix, "grp", n_grp)
-    chosen = lax.dynamic_index_in_dim(sliced, owner, 0, keepdims=False)
-    prefix = gather_by_a2a(chosen, "shard", n_shard).reshape(-1, chosen.shape[-1])
     d = tokens.shape[1]
     pos = arrived[:, d].astype(jnp.int32) * 32 + arrived[:, d + 1].astype(jnp.int32)
     onehot = (jnp.arange(tok_dev, dtype=jnp.int32)[:, None] == pos[None, :]).astype(jnp.bfloat16)
@@ -111,17 +112,15 @@
 
     d = w_qkv.shape[0]
     kh = d // 2
+    w_mine = lax.dynamic_slice_in_dim(w_qkv, core * kh, kh, axis=0)
+    w_rows = lax.all_gather(w_mine, "shard", axis=1, tiled=True)
+    n_mine = lax.dynamic_slice_in_dim(normed, core * kh, kh, axis=1)
+    acc = jnp.dot(n_mine, w_rows, preferred_element_type=jnp.float32)
     kc = kh // 2
-    acc = None
     for part in range(2):
-        w_part = lax.dynamic_slice_in_dim(w_qkv, core * kh + part * kc, kc, axis=0)
-        w_rows = lax.all_gather(w_part, "shard", axis=1, tiled=True)
-        w_other = lax.ppermute(w_rows, "grp", pairs)
-        n_mine = lax.dynamic_slice_in_dim(normed, core * kh + part * kc, kc, axis=1)
+        w_other = lax.ppermute(w_rows[part * kc:(part + 1) * kc], "grp", pairs)
         n_other = lax.dynamic_slice_in_dim(normed, (1 - core) * kh + part * kc, kc, axis=1)
-        term = jnp.dot(n_mine, w_rows, preferred_element_type=jnp.float32)
-        term = term + jnp.dot(n_other, w_other, preferred_element_type=jnp.float32)
-        acc = term if acc is None else acc + term
+        acc = acc + jnp.dot(n_other, w_other, preferred_element_type=jnp.float32)
     qkv = acc.astype(jnp.bfloat16)
 
     lengths = suffix_len.reshape(-1)

time: 243 us -> 212 us (0.87)
  waiting for transfers between devices: 139 us -> 103 us
  local copies, waits for them, and re-layouts: 8.37 us -> 19.9 us
  matrix products: 26.6 us -> 21.6 us
  Pallas kernels: 30.2 us -> 27.2 us
    all_gather x2 -> x1, waiting for transfers between devices: 120 us -> 64.7 us  [shards(): w_rows = lax.all_gather(w_mine, 'shard', axis=1, tiled=True)]
    all_to_all x2, waiting for transfers between devices: 18.4 us -> 38.3 us  [gather_by_a2a(): return lax.all_to_all(spread, axis_name, 0, 0, tiled=True)]
    dot_general x4 -> x3, matrix products: 24.9 us -> 18.2 us  [the longest x2 11 us: shards(): acc = acc + jnp.dot(n_other, w_other, preferred_element_type=jnp.float32)]
    slice x0 -> x2, local copies, waits for them, and re-layouts: none -> 6.65 us  [the longest x1 5.57 us: shards(): w_other = lax.ppermute(w_rows[part * kc:(part + 1) * kc], 'grp', pairs)]
    transpose x0 -> x4, local copies, waits for them, and re-layouts: none -> 6.13 us  [the longest x2 3.37 us: attend(): keys_pre = prefix[:, :HD].T]
    pallas_call x1, Pallas kernels: 30.2 us -> 27.2 us  [attend(): pl.pallas_call(_attn_kernel, out_shape=jax.ShapeDtypeStruct((count, H * H...]
    optimization_barrier x1 -> x0, local copies, waits for them, and re-layouts: 2.76 us -> none  [shards(): local_prefix, arrived = lax.optimization_barrier((prefix_kv[0], arrived))]
    unnamed x9 -> x13, local copies, waits for them, and re-layouts: 0.2 us -> 2.84 us
  transfers between devices with their start and end apart: 7 -> 6, of which waited for: 4 -> 3; matrix products, arithmetic and copies ran while one was open for 16% -> 17% of each run, Pallas kernels for 0% -> 0%
where the time goes in v1:
time: 212 us; the launch traced here: 211 us
  waiting for transfers between devices  103 us (49%)
  Pallas kernels  27.2 us (13%)
  matrix products  21.6 us (10%)
  local copies, waits for them, and re-layouts  19.9 us (9%)
  starting transfers between devices  18.3 us (9%)
  between operations  14.8 us (7%)
  other arithmetic  6.3 us (3%)
    all_gather x1, waiting for transfers between devices, shards(): w_rows = lax.all_gather(w_mine, 'shard', axis=1, tiled=True)  64.7 us
    all_to_all x2, waiting for transfers between devices, gather_by_a2a(): return lax.all_to_all(spread, axis_name, 0, 0, tiled=True)  38.3 us
    pallas_call x1, Pallas kernels, attend(): pl.pallas_call(_attn_kernel, out_shape=jax.ShapeDtypeStruct((count, H * H...  27.2 us
    dot_general x2, matrix products, shards(): acc = acc + jnp.dot(n_other, w_other, preferred_element_type=jnp.float32)  11 us
    all_to_all x2, starting transfers between devices, gather_by_a2a(): return lax.all_to_all(spread, axis_name, 0, 0, tiled=True)  9.91 us
    all_to_all x1, starting transfers between devices, shards(): lax.all_to_all(jnp.concatenate([tokens, code], axis=1), 'shard', 0, 0, ti...  7.92 us
    dot_general x1, matrix products, shards(): acc = jnp.dot(n_mine, w_rows, preferred_element_type=jnp.float32)  7.14 us
    slice x1, local copies, waits for them, and re-layouts, shards(): w_other = lax.ppermute(w_rows[part * kc:(part + 1) * kc], 'grp', pairs)  5.57 us
  transfers between devices with their start and end apart: 6, of which 3 were waited for; matrix products, arithmetic and copies ran while one was open for 17% of the time, Pallas kernels for 0%

profile of v1, /device:TPU:0, one launch (start us, length us, event | category | flops | bytes accessed | tf_op | source)
XLA Modules:
  0.0 211.3 jit_solution(14181602642436231558)
XLA Ops:
  6.5 0.0 copy-start
  6.5 0.0 copy-start.4
  6.5 0.0 all-gather.2.cloned.1.call-start
  6.5 1.2 copy-done
  7.7 0.8 constant_dynamic-slice_fusion
  8.5 0.0 all-gather.2.cloned.1.call-update
  8.6 2.0 broadcast_in_dim.9
  10.5 4.6 %all-to-all-start.1 = ((bf16[8,128,512]{2,1,0:T(8,128)(2,1)}), bf16[8,128,512]{2,1,0:T(8,128)(2,1)S(1)}, u32[]{:S(2)}, u32[]{:S(2)}) async-start(bf16[8,128,512]{2,1,0:T(8,128)(2,1)} %broadcast_in_dim.9), calls=%async_computation.1 | async-start | bytes 2097152 | tf_op jit(solution)/shard_map/all_to_all | solution.py:88
  15.1 0.0 copy-done.4
  15.2 0.2 copy.21
  15.4 3.5 %fusion.4 = bf16[512,2688]{1,0:T(8,128)(2,1)} fusion(bf16[512,2]{1,0:T(8,128)(2,1)S(1)} %copy.21, bf16[512,2560]{1,0:T(8,128)(2,1)} %param.7), kind=kLoop, calls=%fused_computation.9 | loop fusion | flops 8257536 | bytes 5376000 | tf_op jit(solution)/shard_map/concatenate | solution.py:106
  18.9 12.2 %all-to-all-done.1 = bf16[8,128,512]{2,1,0:T(8,128)(2,1)S(1)} async-done(((bf16[8,128,512]{2,1,0:T(8,128)(2,1)}), bf16[8,128,512]{2,1,0:T(8,128)(2,1)S(1)}, u32[]{:S(2)}, u32[]{:S(2)}) %all-to-all-start.1) | async-done | bytes 1048608 | tf_op jit(solution)/shard_map/all_to_all | solution.py:88
  31.0 7.9 %all-to-all-start = ((bf16[16,32,2688]{2,1,0:T(8,128)(2,1)}), bf16[16,32,2688]{2,1,0:T(8,128)(2,1)}, u32[]{:S(2)}, u32[]{:S(2)}) async-start(bf16[16,32,2688]{2,1,0:T(8,128)(2,1)} %bitcast.25), calls=%async_computation | async-start | bytes 5505024 | tf_op jit(solution)/shard_map/all_to_all | solution.py:106
  39.0 64.7 %all-gather.2.cloned.1.call-done = bf16[1280,3072]{0,1:T(8,128)(2,1)} async-done(((bf16[1280,192]{0,1:T(8,128)(2,1)}), bf16[1280,3072]{0,1:T(8,128)(2,1)}) %all-gather.2.cloned.1.call-update) | async-done | bytes 7864336 | tf_op jit(solution)/shard_map/all_gather | solution.py:116
  103.7 5.6 %fusion.18 = (bf16[640,3072]{0,1:T(8,128)(2,1)}, bf16[640,3072]{0,1:T(8,128)(2,1)}) fusion(bf16[1280,3072]{0,1:T(8,128)(2,1)} %all-gather.2.cloned.1.call-done), kind=kLoop, calls=%fused_computation.39 | loop fusion | bytes 15728640 | tf_op jit(solution)/shard_map/slice | solution.py:121
  109.3 0.0 collective-permute-start
  110.6 0.0 all-to-all-done
  110.6 1.5 broadcast_in_dim.22
  112.1 5.3 %all-to-all-start.2 = ((bf16[16,128,512]{2,1,0:T(8,128)(2,1)}), bf16[16,128,512]{2,1,0:T(8,128)(2,1)S(1)}, u32[]{:S(2)}, u32[]{:S(2)}) async-start(bf16[16,128,512]{2,1,0:T(8,128)(2,1)} %broadcast_in_dim.22), calls=%async_computation.2 | async-start | bytes 4194304 | tf_op jit(solution)/shard_map/all_to_all | solution.py:88
  117.5 1.1 fusion.19
  118.6 0.1 copy.20
  118.7 0.1 copy.19
  118.8 0.5 collective-permute-start.1
  119.3 0.0 copy-start.3
  119.3 3.5 %fusion.7 = bf16[512,2688]{1,0:T(8,128)(2,1)S(1)} fusion(bf16[512,2688]{1,0:T(8,128)(2,1)} %bitcast.3, s32[512]{0:T(512)S(1)} %bitcast.27), kind=kOutput, calls=%fused_computation.14 | convolution fusion | flops 1409548288 | bytes 5507072 | tf_op jit(solution)/shard_map/dot_general | solution.py:110
  122.7 0.6 fusion.1
  123.3 0.0 copy-done.3
  123.3 2.2 %fusion.3 = bf16[512,2560]{1,0:T(8,128)(2,1)} fusion(f32[2560]{0:T(1024)S(1)} %copy-done.3, f32[512]{0:T(512)S(1)} %add_rsqrt_fusion, bf16[512,2688]{1,0:T(8,128)(2,1)S(1)} %fusion.7), kind=kLoop, calls=%fused_computation.7 | loop fusion | flops 5242880 | bytes 5255168 | tf_op jit(solution)/shard_map/convert_element_type | solution.py:18
  125.5 26.1 %all-to-all-done.2 = bf16[16,128,512]{2,1,0:T(8,128)(2,1)S(1)} async-done(((bf16[16,128,512]{2,1,0:T(8,128)(2,1)}), bf16[16,128,512]{2,1,0:T(8,128)(2,1)S(1)}, u32[]{:S(2)}, u32[]{:S(2)}) %all-to-all-start.2) | async-done | bytes 2097184 | tf_op jit(solution)/shard_map/all_to_all | solution.py:88
  151.6 1.1 slice_bitcast_fusion
  152.7 2.3 %copy.17.pk_ref = bf16[256,2048]{1,0:T(8,128)(2,1)} copy(bf16[256,2048]{0,1:T(8,128)(2,1)} %slice_bitcast_fusion) | data formatting | bytes 2097152 | tf_op jit(solution)/shard_map/transpose | solution.py:54
  155.0 0.0 copy-start.2
  155.0 7.1 %fusion.5 = f32[512,3072]{1,0:T(8,128)S(1)} fusion(bf16[1280,3072]{0,1:T(8,128)(2,1)} %all-gather.2.cloned.1.call-done, bf16[512,2560]{1,0:T(8,128)(2,1)} %fusion.3, s32[]{:T(128)S(6)} %select_n.68), kind=kOutput, calls=%fused_computation.10 | convolution fusion | flops 4026531840 | bytes 15466500 | tf_op jit(solution)/shard_map/dot_general | solution.py:118
  162.2 0.0 collective-permute-done
  162.2 0.0 copy-done.2
  162.2 4.8 %fusion.9 = f32[512,3072]{1,0:T(8,128)S(1)} fusion(bf16[640,3072]{0,1:T(8,128)(2,1)} %collective-permute-done, bf16[512,2560]{1,0:T(8,128)(2,1)S(1)} %copy-done.2, s32[]{:T(128)S(6)} %select_n.69), kind=kOutput, calls=%fused_computation.16 | convolution fusion | flops 2013265920 | bytes 10878980 | tf_op jit(solution)/shard_map/dot_general | solution.py:123
  167.0 0.0 collective-permute-done.1
  167.0 6.3 %add_convert_fusion.q_ref.sv_ref = bf16[512,3072]{1,0:T(8,128)(2,1)} fusion(f32[512,3072]{1,0:T(8,128)S(1)} %fusion.5, f32[512,3072]{1,0:T(8,128)S(1)} %fusion.9, bf16[640,3072]{0,1:T(8,128)(2,1)} %collective-permute-done.1, bf16[512,2560]{1,0:T(8,128)(2,1)S(1)} %copy-done.2, s32[]{:T(128)S(6)} %select_n.70), kind=kOutput, calls=%fused_computation.2 | convolution fusion | flops 2017984512 | bytes 20316164 | tf_op jit(solution)/shard_map/dot_general | solution.py:123
  173.2 1.7 slice_bitcast_fusion.1
  174.9 1.1 copy.18.sk_ref
  176.0 0.0 copy-start.1
  176.0 1.2 copy-done.1
  177.2 27.2 %shard_map.73 = bf16[512,2560]{1,0:T(8,128)(2,1)} custom-call(s32[1]{0:T(128)} %bitcast.22.len_ref, bf16[512,3072]{1,0:T(8,128)(2,1)} %add_convert_fusion.q_ref.sv_ref, bf16[256,2048]{1,0:T(8,128)(2,1)S(1)} %copy-done.1, bf16[2048,512]{1,0:T(8,128)(2,1)S(1)} %bitcast.24, bf16[256,512]{1,0:T(8,128)(2,1)S(1)} %copy.18.sk_ref, ...), custom_call_target="tpu_custom_call" | custom-call | flops 11408506880 | bytes 7864320 | tf_op jit(solution)/shard_map/pallas_call | solution.py:73
  (6 shorter events, 0.1 us)
Async XLA Ops:
  6.5 1.2 copy-start
  6.5 8.6 %copy-start.4 = (s32[1,512]{1,0:T(1,128)S(1)}, s32[1,512]{1,0:T(1,128)}, u32[]{:S(2)}) copy-start(s32[1,512]{1,0:T(1,128)} %param.13) | copy-start | bytes 6148
  6.5 97.2 %all-gather.2.cloned.1.call-start = ((), (), s32[]{:S(2)}) async-start(), calls=%async_computation.3 | async-start | bytes 8355840 | tf_op jit(solution)/shard_map/all_gather | solution.py:116
  10.5 20.5 %all-to-all-start.1 = ((bf16[8,128,512]{2,1,0:T(8,128)(2,1)}), bf16[8,128,512]{2,1,0:T(8,128)(2,1)S(1)}, u32[]{:S(2)}, u32[]{:S(2)}) async-start(bf16[8,128,512]{2,1,0:T(8,128)(2,1)} %broadcast_in_dim.9), calls=%async_computation.1 | async-start | bytes 2097152 | tf_op jit(solution)/shard_map/all_to_all | solution.py:88
  31.0 79.6 %all-to-all-start = ((bf16[16,32,2688]{2,1,0:T(8,128)(2,1)}), bf16[16,32,2688]{2,1,0:T(8,128)(2,1)}, u32[]{:S(2)}, u32[]{:S(2)}) async-start(bf16[16,32,2688]{2,1,0:T(8,128)(2,1)} %bitcast.25), calls=%async_computation | async-start | bytes 5505024 | tf_op jit(solution)/shard_map/all_to_all | solution.py:106
  109.3 52.9 %collective-permute-start = (bf16[640,3072]{0,1:T(8,128)(2,1)}, bf16[640,3072]{0,1:T(8,128)(2,1)}, u32[]{:S(2)}, u32[]{:S(2)}) collective-permute-start(bf16[640,3072]{0,1:T(8,128)(2,1)} %get-tuple-element.8), channel_id=1, source_target_pairs={{0,16},{16,0},{32,48},{48,32},{64,80},{80,64},{96,112},{112,96},{1... | collective-permute-start | bytes 11796488 | tf_op jit(solution)/shard_map/ppermute | solution.py:121
  112.1 39.5 %all-to-all-start.2 = ((bf16[16,128,512]{2,1,0:T(8,128)(2,1)}), bf16[16,128,512]{2,1,0:T(8,128)(2,1)S(1)}, u32[]{:S(2)}, u32[]{:S(2)}) async-start(bf16[16,128,512]{2,1,0:T(8,128)(2,1)} %broadcast_in_dim.22), calls=%async_computation.2 | async-start | bytes 4194304 | tf_op jit(solution)/shard_map/all_to_all | solution.py:88
  118.8 48.2 %collective-permute-start.1 = (bf16[640,3072]{0,1:T(8,128)(2,1)}, bf16[640,3072]{0,1:T(8,128)(2,1)}, u32[]{:S(2)}, u32[]{:S(2)}) collective-permute-start(bf16[640,3072]{0,1:T(8,128)(2,1)} %get-tuple-element.7), channel_id=1, source_target_pairs={{0,16},{16,0},{32,48},{48,32},{64,80},{80,64},{96,112},{112,96},{1... | collective-permute-start | bytes 11796488 | tf_op jit(solution)/shard_map/ppermute | solution.py:121
  119.3 4.1 %copy-start.3 = (f32[2560]{0:T(1024)S(1)}, f32[2560]{0:T(1024)}, u32[]{:S(2)}) copy-start(f32[2560]{0:T(1024)} %param.8) | copy-start | bytes 30724
  155.0 7.2 %copy-start.2 = (bf16[512,2560]{1,0:T(8,128)(2,1)S(1)}, bf16[512,2560]{1,0:T(8,128)(2,1)}, u32[]{:S(2)}) copy-start(bf16[512,2560]{1,0:T(8,128)(2,1)} %fusion.3) | copy-start | bytes 7864324
  176.0 1.2 copy-start.1
Sparse Core Ops, SparseCore 0:
  9.5 94.1 all-gather.1

commit v2 on v0

--- a/solution.py
+++ b/solution.py
@@ -94,15 +94,15 @@
     core = lax.axis_index("grp") % 2
     pairs = [(g, g ^ 1) for g in range(n_grp)]
 
+    owner = prefix_owner[0]
+    sliced = gather_by_a2a(prefix_kv[0], "grp", n_grp)
+    chosen = lax.dynamic_index_in_dim(sliced, owner, 0, keepdims=False)
+    prefix = gather_by_a2a(chosen, "shard", n_shard).reshape(-1, chosen.shape[-1])
+
     here = slots.reshape(tok_dev, 1) % tok_dev
     code = jnp.concatenate([here // 32, here % 32], axis=1).astype(tokens.dtype)
     code = jnp.pad(code, ((0, 0), (0, 126)))
     arrived = lax.all_to_all(jnp.concatenate([tokens, code], axis=1), "shard", 0, 0, tiled=True)
-    local_prefix, arrived = lax.optimization_barrier((prefix_kv[0], arrived))
-    owner = prefix_owner[0]
-    sliced = gather_by_a2a(local_prefix, "grp", n_grp)
-    chosen = lax.dynamic_index_in_dim(sliced, owner, 0, keepdims=False)
-    prefix = gather_by_a2a(chosen, "shard", n_shard).reshape(-1, chosen.shape[-1])
     d = tokens.shape[1]
     pos = arrived[:, d].astype(jnp.int32) * 32 + arrived[:, d + 1].astype(jnp.int32)
     onehot = (jnp.arange(tok_dev, dtype=jnp.int32)[:, None] == pos[None, :]).astype(jnp.bfloat16)
@@ -110,18 +110,22 @@
     normed = normalize(placed, gain)
 
     d = w_qkv.shape[0]
-    kh = d // 2
-    kc = kh // 2
-    acc = None
-    for part in range(2):
-        w_part = lax.dynamic_slice_in_dim(w_qkv, core * kh + part * kc, kc, axis=0)
-        w_rows = lax.all_gather(w_part, "shard", axis=1, tiled=True)
-        w_other = lax.ppermute(w_rows, "grp", pairs)
-        n_mine = lax.dynamic_slice_in_dim(normed, core * kh + part * kc, kc, axis=1)
-        n_other = lax.dynamic_slice_in_dim(normed, (1 - core) * kh + part * kc, kc, axis=1)
-        term = jnp.dot(n_mine, w_rows, preferred_element_type=jnp.float32)
-        term = term + jnp.dot(n_other, w_other, preferred_element_type=jnp.float32)
-        acc = term if acc is None else acc + term
+    nb = n_grp
+    kb = d // nb
+    g = lax.axis_index("grp")
+    w_piece = lax.dynamic_slice_in_dim(w_qkv, g * kb, kb, axis=0)
+    w_block = lax.all_gather(w_piece, "shard", axis=1, tiled=True)
+    same_core = [list(range(c, n_grp, 2)) for c in range(2)]
+    w_rows = lax.all_gather(w_block, "grp", axis=0, tiled=True, axis_index_groups=same_core)
+    w_other = lax.ppermute(w_rows, "grp", pairs)
+    blocks = normed.reshape(tok_dev, nb // 2, 2, kb)
+    n_even = blocks[:, :, 0, :].reshape(tok_dev, d // 2)
+    n_odd = blocks[:, :, 1, :].reshape(tok_dev, d // 2)
+    is0 = core == 0
+    n_mine = jnp.where(is0, n_even, n_odd)
+    n_other = jnp.where(is0, n_odd, n_even)
+    acc = jnp.dot(n_mine, w_rows, preferred_element_type=jnp.float32)
+    acc = acc + jnp.dot(n_other, w_other, preferred_element_type=jnp.float32)
     qkv = acc.astype(jnp.bfloat16)
 
     lengths = suffix_len.reshape(-1)

time: 243 us -> 283 us (1.16)
  waiting for transfers between devices: 139 us -> 179 us
  local copies, waits for them, and re-layouts: 8.37 us -> 16.5 us
  matrix products: 26.6 us -> 19.4 us
    all_to_all x1, waiting for transfers between devices: 0.01 us -> 39.8 us  [shards(): lax.all_to_all(jnp.concatenate([tokens, code], axis=1), 'shard', 0, 0, ti...]
    dot_general x4 -> x2, matrix products: 24.9 us -> 15.9 us  [the longest x1 9.21 us: shards(): acc = acc + jnp.dot(n_other, w_other, preferred_element_type=jnp.float32)]
    all_gather x2, waiting for transfers between devices: 120 us -> 127 us  [the longest x1 78.1 us: shards(): lax.all_gather(w_block, 'grp', axis=0, tiled=True, axis_index_groups=same...]
    all_to_all x2, waiting for transfers between devices: 18.4 us -> 12.2 us  [gather_by_a2a(): return lax.all_to_all(spread, axis_name, 0, 0, tiled=True)]
    convert_element_type x0 -> x1, local copies, waits for them, and re-layouts: none -> 4.46 us  [normalize(): return (rows32 * factor * gain).astype(jnp.bfloat16)]
    all_gather x0 -> x1, local copies, waits for them, and re-layouts: none -> 4.09 us  [shards(): w_block = lax.all_gather(w_piece, 'shard', axis=1, tiled=True)]
    unnamed x9 -> x13, local copies, waits for them, and re-layouts: 0.2 us -> 3.51 us
  transfers between devices with their start and end apart: 7 -> 6, of which waited for: 4 -> 4; matrix products, arithmetic and copies ran while one was open for 16% -> 13% of each run, Pallas kernels for 0% -> 0%
where the time goes in v2:
time: 283 us; the launch traced here: 282 us
  waiting for transfers between devices  179 us (63%)
  Pallas kernels  28.9 us (10%)
  matrix products  19.4 us (7%)
  local copies, waits for them, and re-layouts  16.5 us (6%)
  starting transfers between devices  14.8 us (5%)
  between operations  14.8 us (5%)
  other arithmetic  8.15 us (3%)
    all_gather x1, waiting for transfers between devices, shards(): lax.all_gather(w_block, 'grp', axis=0, tiled=True, axis_index_groups=same...  78.1 us
    all_gather x1, waiting for transfers between devices, shards(): w_block = lax.all_gather(w_piece, 'shard', axis=1, tiled=True)  49 us
    all_to_all x1, waiting for transfers between devices, shards(): lax.all_to_all(jnp.concatenate([tokens, code], axis=1), 'shard', 0, 0, ti...  39.8 us
    pallas_call x1, Pallas kernels, attend(): pl.pallas_call(_attn_kernel, out_shape=jax.ShapeDtypeStruct((count, H * H...  28.9 us
    all_to_all x2, waiting for transfers between devices, gather_by_a2a(): return lax.all_to_all(spread, axis_name, 0, 0, tiled=True)  12.2 us
    dot_general x1, matrix products, shards(): acc = acc + jnp.dot(n_other, w_other, preferred_element_type=jnp.float32)  9.21 us
    all_to_all x2, starting transfers between devices, gather_by_a2a(): return lax.all_to_all(spread, axis_name, 0, 0, tiled=True)  7.71 us
    all_to_all x1, starting transfers between devices, shards(): lax.all_to_all(jnp.concatenate([tokens, code], axis=1), 'shard', 0, 0, ti...  6.99 us
  transfers between devices with their start and end apart: 6, of which 4 were waited for; matrix products, arithmetic and copies ran while one was open for 13% of the time, Pallas kernels for 0%

profile of v2, /device:TPU:0, one launch (start us, length us, event | category | flops | bytes accessed | tf_op | source)
XLA Modules:
  0.0 281.8 jit_solution(248329554475732467)
XLA Ops:
  6.5 0.0 copy-start
  6.5 0.0 all-gather.3.cloned.1.call-start
  6.5 1.2 copy-done
  7.7 0.8 constant_dynamic-slice_fusion
  8.5 0.0 all-gather.3.cloned.1.call-update
  8.5 0.0 copy-start.2
  8.5 0.0 all-gather.5.cloned.1.call-start
  8.6 49.0 %all-gather.3.cloned.1.call-done = bf16[320,3072]{0,1:T(8,128)(2,1)} async-done(((bf16[320,192]{0,1:T(8,128)(2,1)}), bf16[320,3072]{0,1:T(8,128)(2,1)}) %all-gather.3.cloned.1.call-update) | async-done | bytes 1966096 | tf_op jit(solution)/shard_map/all_gather | solution.py:117
  57.6 4.1 %copy.24 = bf16[320,3072]{1,0:T(8,128)(2,1)} copy(bf16[320,3072]{0,1:T(8,128)(2,1)} %all-gather.3.cloned.1.call-done) | data formatting | bytes 3932160 | tf_op jit(solution)/shard_map/all_gather | solution.py:117
  61.7 0.0 copy-start.4
  61.7 0.0 all-gather.5.cloned.1.call-update
  61.7 78.1 %all-gather.5.cloned.1.call-done = bf16[1280,3072]{1,0:T(8,128)(2,1)} async-done(((bf16[320,3072]{1,0:T(8,128)(2,1)}), bf16[1280,3072]{1,0:T(8,128)(2,1)}) %all-gather.5.cloned.1.call-update) | async-done | bytes 7864336 | tf_op jit(solution)/shard_map/all_gather | solution.py:119
  139.9 0.0 collective-permute-start
  139.9 0.0 copy-done.2
  139.9 1.1 broadcast_in_dim.9
  141.0 4.0 %all-to-all-start.1 = ((bf16[8,128,512]{2,1,0:T(8,128)(2,1)}), bf16[8,128,512]{2,1,0:T(8,128)(2,1)S(1)}, u32[]{:S(2)}, u32[]{:S(2)}) async-start(bf16[8,128,512]{2,1,0:T(8,128)(2,1)} %broadcast_in_dim.9), calls=%async_computation.1 | async-start | bytes 2097152 | tf_op jit(solution)/shard_map/all_to_all | solution.py:87
  145.0 0.0 copy-done.4
  145.0 0.2 copy.27
  145.2 3.5 %fusion.4 = bf16[512,2688]{1,0:T(8,128)(2,1)} fusion(bf16[512,2]{1,0:T(8,128)(2,1)S(1)} %copy.27, bf16[512,2560]{1,0:T(8,128)(2,1)} %param.7), kind=kLoop, calls=%fused_computation.9 | loop fusion | flops 8257536 | bytes 5376000 | tf_op jit(solution)/shard_map/concatenate | solution.py:105
  148.7 12.2 %all-to-all-done.1 = bf16[8,128,512]{2,1,0:T(8,128)(2,1)S(1)} async-done(((bf16[8,128,512]{2,1,0:T(8,128)(2,1)}), bf16[8,128,512]{2,1,0:T(8,128)(2,1)S(1)}, u32[]{:S(2)}, u32[]{:S(2)}) %all-to-all-start.1) | async-done | bytes 1048608 | tf_op jit(solution)/shard_map/all_to_all | solution.py:87
  160.9 7.0 %all-to-all-start = ((bf16[16,32,2688]{2,1,0:T(8,128)(2,1)}), bf16[16,32,2688]{2,1,0:T(8,128)(2,1)}, u32[]{:S(2)}, u32[]{:S(2)}) async-start(bf16[16,32,2688]{2,1,0:T(8,128)(2,1)} %bitcast.25), calls=%async_computation | async-start | bytes 5505024 | tf_op jit(solution)/shard_map/all_to_all | solution.py:105
  169.2 39.8 %all-to-all-done = bf16[16,32,2688]{2,1,0:T(8,128)(2,1)} async-done(((bf16[16,32,2688]{2,1,0:T(8,128)(2,1)}), bf16[16,32,2688]{2,1,0:T(8,128)(2,1)}, u32[]{:S(2)}, u32[]{:S(2)}) %all-to-all-start) | async-done | bytes 2752544 | tf_op jit(solution)/shard_map/all_to_all | solution.py:105
  209.0 1.5 broadcast_in_dim.22
  210.5 3.7 %all-to-all-start.2 = ((bf16[16,128,512]{2,1,0:T(8,128)(2,1)}), bf16[16,128,512]{2,1,0:T(8,128)(2,1)S(1)}, u32[]{:S(2)}, u32[]{:S(2)}) async-start(bf16[16,128,512]{2,1,0:T(8,128)(2,1)} %broadcast_in_dim.22), calls=%async_computation.2 | async-start | bytes 4194304 | tf_op jit(solution)/shard_map/all_to_all | solution.py:87
  214.2 1.1 fusion.10
  215.3 0.1 copy.25
  215.4 0.1 copy.26
  215.6 0.0 copy-start.3
  215.6 3.5 %fusion.5 = bf16[512,2688]{1,0:T(8,128)(2,1)S(1)} fusion(bf16[512,2688]{1,0:T(8,128)(2,1)} %bitcast.3, s32[512]{0:T(512)S(1)} %bitcast.30), kind=kOutput, calls=%fused_computation.13 | convolution fusion | flops 1409548288 | bytes 5507072 | tf_op jit(solution)/shard_map/dot_general | solution.py:109
  219.0 0.6 fusion.1
  219.6 0.0 copy-done.3
  219.6 2.2 fusion.3
  221.8 4.5 %copy.23 = bf16[512,2560]{0,1:T(8,128)(2,1)} copy(bf16[512,2560]{1,0:T(8,128)(2,1)} %fusion.3) | data formatting | bytes 5242880 | tf_op jit(solution)/shard_map/convert_element_type | solution.py:18
  226.3 1.9 broadcast_select_fusion
  228.1 6.7 %fusion.11 = f32[512,3072]{1,0:T(8,128)S(1)} fusion(bf16[512,1280]{0,1:T(8,128)(2,1)S(1)} %bitcast.28, bf16[1280,3072]{1,0:T(8,128)(2,1)} %all-gather.5.cloned.1.call-done), kind=kOutput, calls=%fused_computation.32 | convolution fusion | flops 4026531840 | bytes 15466496 | tf_op jit(solution)/shard_map/dot_general | solution.py:127
  234.9 0.0 collective-permute-done
  234.9 9.2 %add_convert_fusion.q_ref.sk_ref.sv_ref = bf16[512,3072]{1,0:T(8,128)(2,1)} fusion(f32[512,3072]{1,0:T(8,128)S(1)} %fusion.11, bf16[512,1280]{0,1:T(8,128)(2,1)S(1)} %bitcast.27, bf16[1280,3072]{1,0:T(8,128)(2,1)} %collective-permute-done), kind=kOutput, calls=%fused_computation.2 | convolution fusion | flops 4029677568 | bytes 18612224 | tf_op jit(solution)/shard_map/dot_general | solution.py:128
  244.1 0.0 all-to-all-done.2
  244.1 0.0 copy-start.1
  244.1 1.9 copy-done.1
  246.0 28.9 %shard_map.73 = bf16[512,2560]{1,0:T(8,128)(2,1)} custom-call(s32[1]{0:T(128)} %bitcast.22.len_ref, bf16[512,3072]{1,0:T(8,128)(2,1)S(1)} %copy-done.1, bf16[2048,512]{1,0:T(8,128)(2,1)S(1)} %bitcast.23, bf16[2048,512]{1,0:T(8,128)(2,1)S(1)} %bitcast.24, bf16[512,3072]{1,0:T(8,128)(2,1)S(1)} %copy-done.1, bf16[512,3072]{1,0:T(8,128)(2,1)S(1)} %copy-done.1), custom_call_target="tpu_custom_call" | custom-call | flops 12079595520 | bytes 7864320 | tf_op jit(solution)/shard_map/pallas_call | solution.py:72
  (6 shorter events, 0.1 us)
Async XLA Ops:
  6.5 1.2 copy-start
  6.5 51.1 %all-gather.3.cloned.1.call-start = ((), (), s32[]{:S(2)}) async-start(), calls=%async_computation.3 | async-start | bytes 2506752 | tf_op jit(solution)/shard_map/all_gather | solution.py:117
  8.5 131.4 %copy-start.2 = (bf16[1,128,512]{2,1,0:T(8,128)(2,1)S(1)}, bf16[1,128,512]{2,1,0:T(8,128)(2,1)}, u32[]{:S(2)}) copy-start(bf16[1,128,512]{2,1,0:T(8,128)(2,1)} %param.10) | copy-start | bytes 393220
  8.5 131.3 %all-gather.5.cloned.1.call-start = ((), (), s32[]{:S(2)}) async-start(), calls=%async_computation.4 | async-start | bytes 9830400 | tf_op jit(solution)/shard_map/all_gather | solution.py:119
  61.7 83.2 %copy-start.4 = (s32[1,512]{1,0:T(1,128)S(1)}, s32[1,512]{1,0:T(1,128)}, u32[]{:S(2)}) copy-start(s32[1,512]{1,0:T(1,128)} %param.13) | copy-start | bytes 6148
  139.9 95.0 %collective-permute-start = (bf16[1280,3072]{1,0:T(8,128)(2,1)}, bf16[1280,3072]{1,0:T(8,128)(2,1)}, u32[]{:S(2)}, u32[]{:S(2)}) collective-permute-start(bf16[1280,3072]{1,0:T(8,128)(2,1)} %all-gather.5.cloned.1.call-done), channel_id=1, source_target_pairs={{0,16},{16,0},{32,48},{48,32},{64,80},{80,64},{96,112},{112,96},{1... | collective-permute-start | bytes 23592968 | tf_op jit(solution)/shard_map/ppermute | solution.py:120
  141.0 19.9 %all-to-all-start.1 = ((bf16[8,128,512]{2,1,0:T(8,128)(2,1)}), bf16[8,128,512]{2,1,0:T(8,128)(2,1)S(1)}, u32[]{:S(2)}, u32[]{:S(2)}) async-start(bf16[8,128,512]{2,1,0:T(8,128)(2,1)} %broadcast_in_dim.9), calls=%async_computation.1 | async-start | bytes 2097152 | tf_op jit(solution)/shard_map/all_to_all | solution.py:87
  160.9 48.1 %all-to-all-start = ((bf16[16,32,2688]{2,1,0:T(8,128)(2,1)}), bf16[16,32,2688]{2,1,0:T(8,128)(2,1)}, u32[]{:S(2)}, u32[]{:S(2)}) async-start(bf16[16,32,2688]{2,1,0:T(8,128)(2,1)} %bitcast.25), calls=%async_computation | async-start | bytes 5505024 | tf_op jit(solution)/shard_map/all_to_all | solution.py:105
  210.5 33.6 %all-to-all-start.2 = ((bf16[16,128,512]{2,1,0:T(8,128)(2,1)}), bf16[16,128,512]{2,1,0:T(8,128)(2,1)S(1)}, u32[]{:S(2)}, u32[]{:S(2)}) async-start(bf16[16,128,512]{2,1,0:T(8,128)(2,1)} %broadcast_in_dim.22), calls=%async_computation.2 | async-start | bytes 4194304 | tf_op jit(solution)/shard_map/all_to_all | solution.py:87
  215.6 4.1 %copy-start.3 = (f32[2560]{0:T(1024)S(1)}, f32[2560]{0:T(1024)}, u32[]{:S(2)}) copy-start(f32[2560]{0:T(1024)} %param.8) | copy-start | bytes 30724
  244.1 1.9 copy-start.1
Sparse Core Ops, SparseCore 0:
  9.5 48.1 all-gather.2
  61.9 77.9 all-gather.4

commit v3 on v2

--- a/solution.py
+++ b/solution.py
@@ -94,8 +94,8 @@
     core = lax.axis_index("grp") % 2
     pairs = [(g, g ^ 1) for g in range(n_grp)]
 
+    sliced = lax.all_gather(prefix_kv[0], "grp", axis=0)
     owner = prefix_owner[0]
-    sliced = gather_by_a2a(prefix_kv[0], "grp", n_grp)
     chosen = lax.dynamic_index_in_dim(sliced, owner, 0, keepdims=False)
     prefix = gather_by_a2a(chosen, "shard", n_shard).reshape(-1, chosen.shape[-1])
 
@@ -110,20 +110,12 @@
     normed = normalize(placed, gain)
 
     d = w_qkv.shape[0]
-    nb = n_grp
-    kb = d // nb
-    g = lax.axis_index("grp")
-    w_piece = lax.dynamic_slice_in_dim(w_qkv, g * kb, kb, axis=0)
-    w_block = lax.all_gather(w_piece, "shard", axis=1, tiled=True)
-    same_core = [list(range(c, n_grp, 2)) for c in range(2)]
-    w_rows = lax.all_gather(w_block, "grp", axis=0, tiled=True, axis_index_groups=same_core)
+    kh = d // 2
+    w_mine = lax.dynamic_slice_in_dim(w_qkv, core * kh, kh, axis=0)
+    w_rows = lax.all_gather(w_mine, "shard", axis=1, tiled=True)
     w_other = lax.ppermute(w_rows, "grp", pairs)
-    blocks = normed.reshape(tok_dev, nb // 2, 2, kb)
-    n_even = blocks[:, :, 0, :].reshape(tok_dev, d // 2)
-    n_odd = blocks[:, :, 1, :].reshape(tok_dev, d // 2)
-    is0 = core == 0
-    n_mine = jnp.where(is0, n_even, n_odd)
-    n_other = jnp.where(is0, n_odd, n_even)
+    n_mine = lax.dynamic_slice_in_dim(normed, core * kh, kh, axis=1)
+    n_other = lax.dynamic_slice_in_dim(normed, (1 - core) * kh, kh, axis=1)
     acc = jnp.dot(n_mine, w_rows, preferred_element_type=jnp.float32)
     acc = acc + jnp.dot(n_other, w_other, preferred_element_type=jnp.float32)
     qkv = acc.astype(jnp.bfloat16)

time: 283 us -> 210 us (0.74)
  waiting for transfers between devices: 179 us -> 121 us
  local copies, waits for them, and re-layouts: 16.5 us -> 8.58 us
  starting transfers between devices: 14.8 us -> 9.41 us
    all_gather x2, waiting for transfers between devices: 127 us -> 97 us  [the longest x1 72.1 us: shards(): w_rows = lax.all_gather(w_mine, 'shard', axis=1, tiled=True)]
    all_to_all x1, waiting for transfers between devices: 39.8 us -> 15.9 us  [shards(): lax.all_to_all(jnp.concatenate([tokens, code], axis=1), 'shard', 0, 0, ti...]
    all_to_all x2 -> x1, waiting for transfers between devices: 12.2 us -> 7.5 us  [gather_by_a2a(): return lax.all_to_all(spread, axis_name, 0, 0, tiled=True)]
    convert_element_type x1 -> x0, local copies, waits for them, and re-layouts: 4.46 us -> none  [normalize(): return (rows32 * factor * gain).astype(jnp.bfloat16)]
    all_gather x1 -> x0, local copies, waits for them, and re-layouts: 4.09 us -> none  [shards(): w_block = lax.all_gather(w_piece, 'shard', axis=1, tiled=True)]
    all_to_all x2 -> x1, starting transfers between devices: 7.71 us -> 4.06 us  [gather_by_a2a(): return lax.all_to_all(spread, axis_name, 0, 0, tiled=True)]
  transfers between devices with their start and end apart: 6 -> 5, of which waited for: 4 -> 4; matrix products, arithmetic and copies ran while one was open for 13% -> 14% of each run, Pallas kernels for 0% -> 0%
where the time goes in v3:
time: 210 us; the launch traced here: 209 us
  waiting for transfers between devices  121 us (58%)
  Pallas kernels  28.9 us (14%)
  matrix products  19.6 us (9%)
  between operations  16.3 us (8%)
  starting transfers between devices  9.41 us (4%)
  local copies, waits for them, and re-layouts  8.58 us (4%)
  other arithmetic  5.44 us (3%)
    all_gather x1, waiting for transfers between devices, shards(): w_rows = lax.all_gather(w_mine, 'shard', axis=1, tiled=True)  72.1 us
    pallas_call x1, Pallas kernels, attend(): pl.pallas_call(_attn_kernel, out_shape=jax.ShapeDtypeStruct((count, H * H...  28.9 us
    all_gather x1, waiting for transfers between devices, shards(): sliced = lax.all_gather(prefix_kv[0], 'grp', axis=0)  24.9 us
    all_to_all x1, waiting for transfers between devices, shards(): lax.all_to_all(jnp.concatenate([tokens, code], axis=1), 'shard', 0, 0, ti...  15.9 us
    dot_general x1, matrix products, shards(): acc = acc + jnp.dot(n_other, w_other, preferred_element_type=jnp.float32)  9.87 us
    all_to_all x1, waiting for transfers between devices, gather_by_a2a(): return lax.all_to_all(spread, axis_name, 0, 0, tiled=True)  7.5 us
    dot_general x1, matrix products, shards(): acc = jnp.dot(n_mine, w_rows, preferred_element_type=jnp.float32)  6.13 us
    all_to_all x1, starting transfers between devices, shards(): lax.all_to_all(jnp.concatenate([tokens, code], axis=1), 'shard', 0, 0, ti...  5.3 us
  transfers between devices with their start and end apart: 5, of which 4 were waited for; matrix products, arithmetic and copies ran while one was open for 14% of the time, Pallas kernels for 0%

profile of v3, /device:TPU:0, one launch (start us, length us, event | category | flops | bytes accessed | tf_op | source)
XLA Modules:
  0.0 209.2 jit_solution(9112896903301035930)
XLA Ops:
  7.4 0.0 copy-start
  7.4 0.0 all-gather.3.cloned.1.call-start
  7.4 1.2 copy-done
  8.6 0.8 constant_dynamic-slice_fusion
  9.4 0.0 all-gather.3.cloned.1.call-update
  9.4 72.1 %all-gather.3.cloned.1.call-done = bf16[1280,3072]{0,1:T(8,128)(2,1)} async-done(((bf16[1280,192]{0,1:T(8,128)(2,1)}), bf16[1280,3072]{0,1:T(8,128)(2,1)}) %all-gather.3.cloned.1.call-update) | async-done | bytes 7864336 | tf_op jit(solution)/shard_map/all_gather | solution.py:115
  81.5 0.0 collective-permute-start
  81.5 0.7 fusion.12
  82.2 0.2 copy.18
  82.4 3.4 %fusion.4 = bf16[512,2688]{1,0:T(8,128)(2,1)} fusion(bf16[512,2]{1,0:T(8,128)(2,1)S(1)} %copy.18, bf16[512,2560]{1,0:T(8,128)(2,1)} %param.7), kind=kLoop, calls=%fused_computation.9 | loop fusion | flops 8257536 | bytes 5376000 | tf_op jit(solution)/shard_map/concatenate | solution.py:105
  85.8 5.3 %all-to-all-start = ((bf16[16,32,2688]{2,1,0:T(8,128)(2,1)}), bf16[16,32,2688]{2,1,0:T(8,128)(2,1)}, u32[]{:S(2)}, u32[]{:S(2)}) async-start(bf16[16,32,2688]{2,1,0:T(8,128)(2,1)} %bitcast.19), calls=%async_computation | async-start | bytes 5505024 | tf_op jit(solution)/shard_map/all_to_all | solution.py:105
  91.1 0.0 all-gather.5.cloned.1.call-start
  91.2 0.5 all-gather.5.cloned.1.call-update
  93.0 24.9 %all-gather.5.cloned.1.call-done = bf16[8,128,512]{2,1,0:T(8,128)(2,1)} async-done(((bf16[1,128,512]{2,1,0:T(8,128)(2,1)}), bf16[8,128,512]{2,1,0:T(8,128)(2,1)}) %all-gather.5.cloned.1.call-update) | async-done | bytes 1048592 | tf_op jit(solution)/shard_map/all_gather | solution.py:97
  118.0 0.9 dynamic-slice_bitcast_fusion
  118.9 15.9 %all-to-all-done = bf16[16,32,2688]{2,1,0:T(8,128)(2,1)} async-done(((bf16[16,32,2688]{2,1,0:T(8,128)(2,1)}), bf16[16,32,2688]{2,1,0:T(8,128)(2,1)}, u32[]{:S(2)}, u32[]{:S(2)}) %all-to-all-start) | async-done | bytes 2752544 | tf_op jit(solution)/shard_map/all_to_all | solution.py:105
  134.8 1.5 broadcast_in_dim.5
  136.3 4.1 %all-to-all-start.1 = ((bf16[16,128,512]{2,1,0:T(8,128)(2,1)}), bf16[16,128,512]{2,1,0:T(8,128)(2,1)S(1)}, u32[]{:S(2)}, u32[]{:S(2)}) async-start(bf16[16,128,512]{2,1,0:T(8,128)(2,1)} %broadcast_in_dim.5), calls=%async_computation.1 | async-start | bytes 4194304 | tf_op jit(solution)/shard_map/all_to_all | solution.py:87
  140.4 1.1 fusion.15
  141.5 0.1 copy.16
  141.6 0.1 copy.17
  141.7 0.0 copy-start.2
  141.7 0.0 slice-start
  141.7 3.6 %fusion.8 = bf16[512,2688]{1,0:T(8,128)(2,1)S(1)} fusion(bf16[512,2688]{1,0:T(8,128)(2,1)} %bitcast.3, s32[512]{0:T(512)S(1)} %bitcast.20), kind=kOutput, calls=%fused_computation.14 | convolution fusion | flops 1409548288 | bytes 5507072 | tf_op jit(solution)/shard_map/dot_general | solution.py:109
  145.4 0.0 slice-start.1
  145.4 0.6 fusion.1
  146.0 0.0 copy-done.2
  146.0 0.7 fusion.3
  146.6 0.0 slice-done
  146.6 0.7 slice-done.1
  147.4 6.1 %fusion.6 = f32[512,3072]{1,0:T(8,128)} fusion(bf16[1280,3072]{0,1:T(8,128)(2,1)S(1)} %bitcast.22, bf16[512,2560]{1,0:T(8,128)(2,1)S(1)} %fusion.3, s32[]{:T(128)S(6)} %select_n.65), kind=kOutput, calls=%fused_computation.11 | convolution fusion | flops 4026531840 | bytes 15466500 | tf_op jit(solution)/shard_map/dot_general | solution.py:119
  153.5 0.0 collective-permute-done
  153.5 9.9 %add_convert_fusion.q_ref.sk_ref.sv_ref = bf16[512,3072]{1,0:T(8,128)(2,1)} fusion(f32[512,3072]{1,0:T(8,128)} %fusion.6, bf16[1280,3072]{0,1:T(8,128)(2,1)} %collective-permute-done, bf16[512,2560]{1,0:T(8,128)(2,1)S(1)} %fusion.3, s32[]{:T(128)S(6)} %select_n.66), kind=kOutput, calls=%fused_computation.2 | convolution fusion | flops 4029677568 | bytes 18612228 | tf_op jit(solution)/shard_map/dot_general | solution.py:120
  163.4 7.5 %all-to-all-done.1 = bf16[16,128,512]{2,1,0:T(8,128)(2,1)S(1)} async-done(((bf16[16,128,512]{2,1,0:T(8,128)(2,1)}), bf16[16,128,512]{2,1,0:T(8,128)(2,1)S(1)}, u32[]{:S(2)}, u32[]{:S(2)}) %all-to-all-start.1) | async-done | bytes 2097184 | tf_op jit(solution)/shard_map/all_to_all | solution.py:87
  170.9 0.0 copy-start.1
  170.9 1.9 copy-done.1
  172.8 28.9 %shard_map.73 = bf16[512,2560]{1,0:T(8,128)(2,1)} custom-call(s32[1]{0:T(128)} %bitcast.16.len_ref, bf16[512,3072]{1,0:T(8,128)(2,1)S(1)} %copy-done.1, bf16[2048,512]{1,0:T(8,128)(2,1)S(1)} %bitcast.17, bf16[2048,512]{1,0:T(8,128)(2,1)S(1)} %bitcast.18, bf16[512,3072]{1,0:T(8,128)(2,1)S(1)} %copy-done.1, bf16[512,3072]{1,0:T(8,128)(2,1)S(1)} %copy-done.1), custom_call_target="tpu_custom_call" | custom-call | flops 12079595520 | bytes 7864320 | tf_op jit(solution)/shard_map/pallas_call | solution.py:72
  (5 shorter events, 0.0 us)
Async XLA Ops:
  7.4 1.2 copy-start
  7.4 74.1 %all-gather.3.cloned.1.call-start = ((), (), s32[]{:S(2)}) async-start(), calls=%async_computation.2 | async-start | bytes 8355840 | tf_op jit(solution)/shard_map/all_gather | solution.py:115
  81.5 72.1 %collective-permute-start = (bf16[1280,3072]{0,1:T(8,128)(2,1)}, bf16[1280,3072]{0,1:T(8,128)(2,1)}, u32[]{:S(2)}, u32[]{:S(2)}) collective-permute-start(bf16[1280,3072]{0,1:T(8,128)(2,1)} %all-gather.3.cloned.1.call-done), channel_id=1, source_target_pairs={{0,16},{16,0},{32,48},{48,32},{64,80},{80,64},{96,112},{112,96},{1... | collective-permute-start | bytes 23592968 | tf_op jit(solution)/shard_map/ppermute | solution.py:116
  85.8 49.0 %all-to-all-start = ((bf16[16,32,2688]{2,1,0:T(8,128)(2,1)}), bf16[16,32,2688]{2,1,0:T(8,128)(2,1)}, u32[]{:S(2)}, u32[]{:S(2)}) async-start(bf16[16,32,2688]{2,1,0:T(8,128)(2,1)} %bitcast.19), calls=%async_computation | async-start | bytes 5505024 | tf_op jit(solution)/shard_map/all_to_all | solution.py:105
  91.1 26.8 %all-gather.5.cloned.1.call-start = ((), (), s32[]{:S(2)}) async-start(), calls=%async_computation.3 | async-start | bytes 1179648 | tf_op jit(solution)/shard_map/all_gather | solution.py:97
  136.3 34.6 %all-to-all-start.1 = ((bf16[16,128,512]{2,1,0:T(8,128)(2,1)}), bf16[16,128,512]{2,1,0:T(8,128)(2,1)S(1)}, u32[]{:S(2)}, u32[]{:S(2)}) async-start(bf16[16,128,512]{2,1,0:T(8,128)(2,1)} %broadcast_in_dim.5), calls=%async_computation.1 | async-start | bytes 4194304 | tf_op jit(solution)/shard_map/all_to_all | solution.py:87
  141.7 4.2 %copy-start.2 = (f32[2560]{0:T(1024)S(1)}, f32[2560]{0:T(1024)}, u32[]{:S(2)}) copy-start(f32[2560]{0:T(1024)} %param.8) | copy-start | bytes 30724
  141.7 4.9 %slice-start = ((s8[7864320]{0:T(1024)(128)(4,1)}), s8[4194304]{0:T(1024)(128)(4,1)S(1)}, s32[]{:S(2)}) async-start(s8[7864320]{0:T(1024)(128)(4,1)} %bitcast.21), calls=%async_computation.4 | async-start | bytes 8388608
  145.4 2.0 slice-start.1
  170.9 1.9 copy-start.1
Sparse Core Ops, SparseCore 0:
  10.3 71.1 all-gather.2
Sparse Core Ops, SparseCore 1:
  93.3 24.6 all-gather.4

commit v4 on v3

--- a/solution.py
+++ b/solution.py
@@ -91,11 +91,9 @@
     tok_dev = tokens.shape[0]
     n_grp = lax.axis_size("grp")
     n_shard = lax.axis_size("shard")
-    core = lax.axis_index("grp") % 2
-    pairs = [(g, g ^ 1) for g in range(n_grp)]
 
-    sliced = lax.all_gather(prefix_kv[0], "grp", axis=0)
     owner = prefix_owner[0]
+    sliced = gather_by_a2a(prefix_kv[0], "grp", n_grp)
     chosen = lax.dynamic_index_in_dim(sliced, owner, 0, keepdims=False)
     prefix = gather_by_a2a(chosen, "shard", n_shard).reshape(-1, chosen.shape[-1])
 
@@ -110,14 +108,13 @@
     normed = normalize(placed, gain)
 
     d = w_qkv.shape[0]
-    kh = d // 2
-    w_mine = lax.dynamic_slice_in_dim(w_qkv, core * kh, kh, axis=0)
-    w_rows = lax.all_gather(w_mine, "shard", axis=1, tiled=True)
-    w_other = lax.ppermute(w_rows, "grp", pairs)
-    n_mine = lax.dynamic_slice_in_dim(normed, core * kh, kh, axis=1)
-    n_other = lax.dynamic_slice_in_dim(normed, (1 - core) * kh, kh, axis=1)
-    acc = jnp.dot(n_mine, w_rows, preferred_element_type=jnp.float32)
-    acc = acc + jnp.dot(n_other, w_other, preferred_element_type=jnp.float32)
+    kb = d // n_grp
+    g = lax.axis_index("grp")
+    w_piece = lax.dynamic_slice_in_dim(w_qkv, g * kb, kb, axis=0)
+    pieces = lax.all_gather(w_piece, ("grp", "shard"), axis=0)
+    pieces = pieces.reshape(n_grp, n_shard, kb, w_qkv.shape[1])
+    acc = jnp.einsum("ngr,gsrc->nsc", normed.reshape(tok_dev, n_grp, kb), pieces,
+                     preferred_element_type=jnp.float32).reshape(tok_dev, -1)
     qkv = acc.astype(jnp.bfloat16)
 
     lengths = suffix_len.reshape(-1)

time: 210 us -> 195 us (0.929)
  waiting for transfers between devices: 121 us -> 93.5 us
  starting transfers between devices: 9.41 us -> 16.7 us
  local copies, waits for them, and re-layouts: 8.58 us -> 13.5 us
    all_gather x2 -> x1, waiting for transfers between devices: 97 us -> 35.7 us  [shards(): pieces = lax.all_gather(w_piece, ('grp', 'shard'), axis=0)]
    all_to_all x1, waiting for transfers between devices: 15.9 us -> 44.9 us  [shards(): lax.all_to_all(jnp.concatenate([tokens, code], axis=1), 'shard', 0, 0, ti...]
    all_to_all x1 -> x2, waiting for transfers between devices: 7.5 us -> 12.8 us  [gather_by_a2a(): return lax.all_to_all(spread, axis_name, 0, 0, tiled=True)]
    convert_element_type x0 -> x1, local copies, waits for them, and re-layouts: none -> 4.48 us  [normalize(): return (rows32 * factor * gain).astype(jnp.bfloat16)]
    all_to_all x1 -> x2, starting transfers between devices: 4.06 us -> 8.3 us  [gather_by_a2a(): return lax.all_to_all(spread, axis_name, 0, 0, tiled=True)]
    all_to_all x1, starting transfers between devices: 5.3 us -> 8.39 us  [shards(): lax.all_to_all(jnp.concatenate([tokens, code], axis=1), 'shard', 0, 0, ti...]
    dot_general x2 -> x1, matrix products: 16 us -> 16.1 us  [shards(): jnp.einsum('ngr,gsrc->nsc', normed.reshape(tok_dev, n_grp, kb), pieces, p...]
    unnamed x13 -> x12, local copies, waits for them, and re-layouts: 4.25 us -> 4.28 us
  transfers between devices with their start and end apart: 5 -> 4, of which waited for: 4 -> 3; matrix products, arithmetic and copies ran while one was open for 14% -> 18% of each run, Pallas kernels for 0% -> 0%
where the time goes in v4:
time: 195 us; the launch traced here: 193 us
  waiting for transfers between devices  93.5 us (48%)
  Pallas kernels  28.9 us (15%)
  matrix products  19.7 us (10%)
  starting transfers between devices  16.7 us (9%)
  between operations  14.8 us (8%)
  local copies, waits for them, and re-layouts  13.5 us (7%)
  other arithmetic  6.3 us (3%)
    all_to_all x1, waiting for transfers between devices, shards(): lax.all_to_all(jnp.concatenate([tokens, code], axis=1), 'shard', 0, 0, ti...  44.9 us
    all_gather x1, waiting for transfers between devices, shards(): pieces = lax.all_gather(w_piece, ('grp', 'shard'), axis=0)  35.7 us
    pallas_call x1, Pallas kernels, attend(): pl.pallas_call(_attn_kernel, out_shape=jax.ShapeDtypeStruct((count, H * H...  28.9 us
    dot_general x1, matrix products, shards(): jnp.einsum('ngr,gsrc->nsc', normed.reshape(tok_dev, n_grp, kb), pieces, p...  16.1 us
    all_to_all x2, waiting for transfers between devices, gather_by_a2a(): return lax.all_to_all(spread, axis_name, 0, 0, tiled=True)  12.8 us
    all_to_all x1, starting transfers between devices, shards(): lax.all_to_all(jnp.concatenate([tokens, code], axis=1), 'shard', 0, 0, ti...  8.39 us
    all_to_all x2, starting transfers between devices, gather_by_a2a(): return lax.all_to_all(spread, axis_name, 0, 0, tiled=True)  8.3 us
    convert_element_type x1, local copies, waits for them, and re-layouts, normalize(): return (rows32 * factor * gain).astype(jnp.bfloat16)  4.48 us
  transfers between devices with their start and end apart: 4, of which 3 were waited for; matrix products, arithmetic and copies ran while one was open for 18% of the time, Pallas kernels for 0%

profile of v4, /device:TPU:0, one launch (start us, length us, event | category | flops | bytes accessed | tf_op | source)
XLA Modules:
  0.0 193.4 jit_solution(4718614057780178570)
XLA Ops:
  6.5 0.0 copy-start
  6.5 0.0 copy-start.3
  6.5 0.0 all-gather.4.cloned.1.call-start
  6.5 1.2 copy-done
  7.7 0.8 dynamic-slice_bitcast_fusion
  8.5 0.0 all-gather.4.cloned.1.call-update
  8.5 2.0 %broadcast_in_dim.9 = bf16[8,128,512]{2,1,0:T(8,128)(2,1)} broadcast(bf16[128,512]{1,0:T(8,128)(2,1)} %bitcast.32), dimensions={1,2} | broadcast | bytes 1179648 | tf_op jit(solution)/shard_map/broadcast_in_dim | solution.py:86
  10.5 4.6 %all-to-all-start.1 = ((bf16[8,128,512]{2,1,0:T(8,128)(2,1)}), bf16[8,128,512]{2,1,0:T(8,128)(2,1)S(1)}, u32[]{:S(2)}, u32[]{:S(2)}) async-start(bf16[8,128,512]{2,1,0:T(8,128)(2,1)} %broadcast_in_dim.9), calls=%async_computation.1 | async-start | bytes 2097152 | tf_op jit(solution)/shard_map/all_to_all | solution.py:87
  15.1 0.0 copy-done.3
  15.2 0.2 copy.30
  15.3 3.5 %fusion.4 = bf16[512,2688]{1,0:T(8,128)(2,1)} fusion(bf16[512,2]{1,0:T(8,128)(2,1)S(1)} %copy.30, bf16[512,2560]{1,0:T(8,128)(2,1)} %param.7), kind=kLoop, calls=%fused_computation.9 | loop fusion | flops 8257536 | bytes 5376000 | tf_op jit(solution)/shard_map/concatenate | solution.py:103
  18.8 12.8 %all-to-all-done.1 = bf16[8,128,512]{2,1,0:T(8,128)(2,1)S(1)} async-done(((bf16[8,128,512]{2,1,0:T(8,128)(2,1)}), bf16[8,128,512]{2,1,0:T(8,128)(2,1)S(1)}, u32[]{:S(2)}, u32[]{:S(2)}) %all-to-all-start.1) | async-done | bytes 1048608 | tf_op jit(solution)/shard_map/all_to_all | solution.py:87
  31.7 8.4 %all-to-all-start = ((bf16[16,32,2688]{2,1,0:T(8,128)(2,1)}), bf16[16,32,2688]{2,1,0:T(8,128)(2,1)}, u32[]{:S(2)}, u32[]{:S(2)}) async-start(bf16[16,32,2688]{2,1,0:T(8,128)(2,1)} %bitcast.30), calls=%async_computation | async-start | bytes 5505024 | tf_op jit(solution)/shard_map/all_to_all | solution.py:103
  41.4 44.9 %all-to-all-done = bf16[16,32,2688]{2,1,0:T(8,128)(2,1)} async-done(((bf16[16,32,2688]{2,1,0:T(8,128)(2,1)}), bf16[16,32,2688]{2,1,0:T(8,128)(2,1)}, u32[]{:S(2)}, u32[]{:S(2)}) %all-to-all-start) | async-done | bytes 2752544 | tf_op jit(solution)/shard_map/all_to_all | solution.py:103
  86.3 1.6 broadcast_in_dim.22
  87.9 3.7 %all-to-all-start.2 = ((bf16[16,128,512]{2,1,0:T(8,128)(2,1)}), bf16[16,128,512]{2,1,0:T(8,128)(2,1)S(1)}, u32[]{:S(2)}, u32[]{:S(2)}) async-start(bf16[16,128,512]{2,1,0:T(8,128)(2,1)} %broadcast_in_dim.22), calls=%async_computation.2 | async-start | bytes 4194304 | tf_op jit(solution)/shard_map/all_to_all | solution.py:87
  91.6 1.1 fusion.10
  92.8 0.1 copy.28
  92.9 0.1 copy.29
  93.0 0.0 copy-start.2
  93.0 3.6 %fusion.5 = bf16[512,2688]{1,0:T(8,128)(2,1)S(1)} fusion(bf16[512,2688]{1,0:T(8,128)(2,1)} %bitcast.3, s32[512]{0:T(512)S(1)} %bitcast.33), kind=kOutput, calls=%fused_computation.11 | convolution fusion | flops 1409548288 | bytes 5507072 | tf_op jit(solution)/shard_map/dot_general | solution.py:107
  96.6 0.6 fusion.1
  97.2 0.0 copy-done.2
  97.2 2.2 %fusion.3 = bf16[512,2560]{1,0:T(8,128)(2,1)} fusion(f32[2560]{0:T(1024)S(1)} %copy-done.2, f32[512]{0:T(512)S(1)} %add_rsqrt_fusion, bf16[512,2688]{1,0:T(8,128)(2,1)S(1)} %fusion.5), kind=kLoop, calls=%fused_computation.7 | loop fusion | flops 5242880 | bytes 5255168 | tf_op jit(solution)/shard_map/convert_element_type | solution.py:18
  99.4 4.5 %copy.23 = bf16[512,2560]{0,1:T(8,128)(2,1)} copy(bf16[512,2560]{1,0:T(8,128)(2,1)} %fusion.3) | data formatting | bytes 5242880 | tf_op jit(solution)/shard_map/convert_element_type | solution.py:18
  103.9 35.7 %all-gather.4.cloned.1.call-done = bf16[128,320,192]{1,2,0:T(8,128)(2,1)} async-done(((bf16[1,320,192]{1,2,0:T(8,128)(2,1)}), bf16[128,320,192]{1,2,0:T(8,128)(2,1)}) %all-gather.4.cloned.1.call-update) | async-done | bytes 15728656 | tf_op jit(solution)/shard_map/all_gather | solution.py:114
  139.6 16.1 %bitcast_convert_fusion.q_ref.sk_ref.sv_ref = bf16[512,3072]{1,0:T(8,128)(2,1)} fusion(bf16[512,8,320]{0,2,1:T(8,128)(2,1)} %bitcast.31, bf16[3072,8,320]{2,0,1:T(8,128)(2,1)} %bitcast.34), kind=kOutput, calls=%fused_computation.2 | convolution fusion | flops 8054636544 | bytes 21495808 | tf_op jit(solution)/shard_map/ngr,gsrc->nsc/dot_general | solution.py:116
  155.7 0.0 all-to-all-done.2
  155.7 0.0 copy-start.1
  155.7 1.9 copy-done.1
  157.6 28.9 %shard_map.73 = bf16[512,2560]{1,0:T(8,128)(2,1)} custom-call(s32[1]{0:T(128)} %bitcast.27.len_ref, bf16[512,3072]{1,0:T(8,128)(2,1)S(1)} %copy-done.1, bf16[2048,512]{1,0:T(8,128)(2,1)S(1)} %bitcast.28, bf16[2048,512]{1,0:T(8,128)(2,1)S(1)} %bitcast.29, bf16[512,3072]{1,0:T(8,128)(2,1)S(1)} %copy-done.1, bf16[512,3072]{1,0:T(8,128)(2,1)S(1)} %copy-done.1), custom_call_target="tpu_custom_call" | custom-call | flops 12079595520 | bytes 7864320 | tf_op jit(solution)/shard_map/pallas_call | solution.py:72
  (6 shorter events, 0.1 us)
Async XLA Ops:
  6.5 1.2 copy-start
  6.5 8.5 %copy-start.3 = (s32[1,512]{1,0:T(1,128)S(1)}, s32[1,512]{1,0:T(1,128)}, u32[]{:S(2)}) copy-start(s32[1,512]{1,0:T(1,128)} %param.13) | copy-start | bytes 6148
  6.5 133.1 %all-gather.4.cloned.1.call-start = ((), (), s32[]{:S(2)}) async-start(), calls=%async_computation.3 | async-start | bytes 19021824 | tf_op jit(solution)/shard_map/all_gather | solution.py:114
  10.5 21.2 %all-to-all-start.1 = ((bf16[8,128,512]{2,1,0:T(8,128)(2,1)}), bf16[8,128,512]{2,1,0:T(8,128)(2,1)S(1)}, u32[]{:S(2)}, u32[]{:S(2)}) async-start(bf16[8,128,512]{2,1,0:T(8,128)(2,1)} %broadcast_in_dim.9), calls=%async_computation.1 | async-start | bytes 2097152 | tf_op jit(solution)/shard_map/all_to_all | solution.py:87
  31.7 54.6 %all-to-all-start = ((bf16[16,32,2688]{2,1,0:T(8,128)(2,1)}), bf16[16,32,2688]{2,1,0:T(8,128)(2,1)}, u32[]{:S(2)}, u32[]{:S(2)}) async-start(bf16[16,32,2688]{2,1,0:T(8,128)(2,1)} %bitcast.30), calls=%async_computation | async-start | bytes 5505024 | tf_op jit(solution)/shard_map/all_to_all | solution.py:103
  87.9 67.8 %all-to-all-start.2 = ((bf16[16,128,512]{2,1,0:T(8,128)(2,1)}), bf16[16,128,512]{2,1,0:T(8,128)(2,1)S(1)}, u32[]{:S(2)}, u32[]{:S(2)}) async-start(bf16[16,128,512]{2,1,0:T(8,128)(2,1)} %broadcast_in_dim.22), calls=%async_computation.2 | async-start | bytes 4194304 | tf_op jit(solution)/shard_map/all_to_all | solution.py:87
  93.0 4.2 %copy-start.2 = (f32[2560]{0:T(1024)S(1)}, f32[2560]{0:T(1024)}, u32[]{:S(2)}) copy-start(f32[2560]{0:T(1024)} %param.8) | copy-start | bytes 30724
  155.7 1.9 copy-start.1
Sparse Core Ops, SparseCore 0:
  10.2 129.3 all-gather.3
